TPU v7x, 32 devices: a whole 2x2x4 slice. The times are simulated.
32 devices in a mesh: track: 4 (over z), cross: 8 (over y, x, core).
Axes of the slice: x: 2, y: 2, z: 4, core: 2. Of those that a mesh axis runs over, the one named last changes fastest.
Arguments:
- cube: bfloat16 [1024, 256, 224], P('track', 'cross'), may hold values from -60 to 113, as said below
Outputs:
- scores: float32 [1024, 256], P('track', 'cross')
Inputs may be any that keep to these rules, and one draw needn't show every extreme that they name: `cube`: A positive radiance level per band plus noise, scaled per band and by position.
All inputs are finite; a program needn't handle non-finite values.
Results may differ from a plain program's by a relative error of at most 0.0003.
Values may be sent and summed in bfloat16 or wider, within the bound.
No kernel may reach another device: no remote copies, remote signals or barrier semaphores. Data moves between devices by JAX's collectives and lax.ppermute only.
A program may use at most 64 MiB of HBM per device.

v0:
```python
import jax
import jax.numpy as jnp
from jax import lax
from jax.sharding import PartitionSpec as P

HALF = 15
LOAD = 0.02


def with_halo(block, sides, width):
    for axis, dim in sides:
        count = lax.axis_size(axis)
        forward = [(i, i + 1) for i in range(count - 1)]
        backward = [(target, source) for source, target in forward]
        low = lax.ppermute(
            lax.slice_in_dim(block, block.shape[dim] - width, None, axis=dim), axis, forward
        )
        high = lax.ppermute(lax.slice_in_dim(block, 0, width, axis=dim), axis, backward)
        block = jnp.concatenate([low, block, high], axis=dim)
    return block


def band_matrix(rows_in, rows_out, dtype):
    source = jnp.arange(rows_in)[:, None]
    target = jnp.arange(rows_out)[None, :]
    inside = (source >= target) & (source <= target + 2 * HALF)
    return inside.astype(dtype)


def window_count(first, local, total):
    index = first + jnp.arange(local)
    upper = jnp.minimum(index + HALF, total - 1)
    lower = jnp.maximum(index - HALF, 0)
    return (upper - lower + 1).astype(jnp.float32)


def sum_pixels(values, width, dtype):
    weights = band_matrix(width + 2 * HALF, width, dtype)
    return jnp.einsum(
        "lqb,qp->lpb", values, weights, precision=None, preferred_element_type=jnp.float32
    )


def sum_lines(values, height, dtype, precision):
    weights = band_matrix(height + 2 * HALF, height, dtype)
    return jnp.einsum(
        "kpb,kl->lpb", values, weights, precision=precision, preferred_element_type=jnp.float32
    )


def shards(cube):
    lines_dev, pix_dev, bands = cube.shape
    n_track = lax.axis_size("track")
    n_cross = lax.axis_size("cross")
    total_lines = lines_dev * n_track
    total_pix = pix_dev * n_cross
    highest = lax.Precision.HIGHEST
    extended = with_halo(cube, (("track", 0), ("cross", 1)), HALF)
    across = sum_pixels(extended, pix_dev, jnp.bfloat16)
    window = sum_lines(across, lines_dev, jnp.float32, highest)
    line_count = window_count(lax.axis_index("track") * lines_dev, lines_dev, total_lines)
    pixel_count = window_count(lax.axis_index("cross") * pix_dev, pix_dev, total_pix)
    count = line_count[:, None, None] * pixel_count[None, :, None]
    residual = cube.astype(jnp.float32) - window / count
    flat = residual.reshape(lines_dev * pix_dev, bands)
    flat_bf = flat.astype(jnp.bfloat16)
    partial_cov = jnp.dot(flat_bf.T, flat_bf, preferred_element_type=jnp.float32)
    covariance = lax.psum(partial_cov, ("track", "cross")) / (total_lines * total_pix)
    identity = jnp.eye(bands, dtype=jnp.float32)
    loaded = covariance + LOAD * (jnp.trace(covariance) / bands) * identity
    factor = jnp.linalg.cholesky(loaded)
    inverse = jax.scipy.linalg.solve_triangular(factor, identity, lower=True)
    whitened = jnp.dot(flat, inverse.T, precision=highest, preferred_element_type=jnp.float32)
    scores = jnp.sum(whitened * whitened, axis=1) / bands
    return scores.reshape(lines_dev, pix_dev)


def solution(mesh):
    return jax.shard_map(
        shards,
        mesh=mesh,
        in_specs=(P("track", "cross", None),),
        out_specs=P("track", "cross"),
        check_vma=False,
    )
```

profile of v0, /device:TPU:1, one launch (start us, length us, event | category | flops | bytes accessed | tf_op | source)
XLA Modules:
  0.0 329.4 jit_solution(2984762335970636967)
XLA Ops:
  6.5 0.0 all-reduce.5.cloned.1.call-start
  6.5 7.8 %copy.6 = bf16[256,32,224]{2,1,0:T(8,128)(2,1)} copy(bf16[256,32,224]{0,2,1:T(8,128)(2,1)} %param.1) | data formatting | bytes 7340032 | tf_op args[0]
  14.4 1.1 fusion.46
  15.5 4.0 %collective-permute-start = (bf16[15,32,224]{2,1,0:T(8,128)(2,1)S(1)}, bf16[15,32,224]{2,1,0:T(8,128)(2,1)S(1)}, u32[]{:S(2)}, u32[]{:S(2)}) collective-permute-start(bf16[15,32,224]{2,1,0:T(8,128)(2,1)S(1)} %get-tuple-element.27), channel_id=1, source_target_pairs={{0,8},{8,16},{16,24},{1,9},{9,17},{17,25},{2,10},{10,18},{18,26},{... | collective-permute-start | bytes 645128 | tf_op jit(solution)/shard_map/ppermute | solution.py:15
  19.5 1.3 collective-permute-start.1
  20.8 3.3 collective-permute-done
  24.1 3.8 %collective-permute-done.1 = bf16[15,32,224]{2,1,0:T(8,128)(2,1)S(1)} collective-permute-done((bf16[15,32,224]{2,1,0:T(8,128)(2,1)S(1)}, bf16[15,32,224]{2,1,0:T(8,128)(2,1)S(1)}, u32[]{:S(2)}, u32[]{:S(2)}) %collective-permute-start.1) | collective-permute-done | bytes 215072 | tf_op jit(solution)/shard_map/ppermute | solution.py:18
  27.9 2.7 pad_maximum_fusion
  30.7 1.0 fusion.45
  31.7 0.8 copy.9
  32.5 4.9 %collective-permute-start.2 = (bf16[286,15,224]{2,0,1:T(8,128)(2,1)S(1)}, bf16[286,15,224]{2,0,1:T(8,128)(2,1)}, u32[]{:S(2)}, u32[]{:S(2)}) collective-permute-start(bf16[286,15,224]{2,0,1:T(8,128)(2,1)S(1)} %copy.9), channel_id=1, source_target_pairs={{0,1},{1,2},{2,3},{3,4},{4,5},{5,6},{6,7},{8,9},{9,10},{10,11},{11... | collective-permute-start | bytes 5765768 | tf_op jit(solution)/shard_map/ppermute | solution.py:15
  37.4 2.1 copy.10
  39.6 1.9 collective-permute-start.3
  41.5 0.0 copy-start.1
  41.6 0.1 broadcast_multiply_fusion.1
  41.6 20.0 %collective-permute-done.2 = bf16[286,15,224]{2,0,1:T(8,128)(2,1)} collective-permute-done((bf16[286,15,224]{2,0,1:T(8,128)(2,1)S(1)}, bf16[286,15,224]{2,0,1:T(8,128)(2,1)}, u32[]{:S(2)}, u32[]{:S(2)}) %collective-permute-start.2) | collective-permute-done | bytes 1921952 | tf_op jit(solution)/shard_map/ppermute | solution.py:15
  61.6 2.9 copy.11
  64.5 22.6 %collective-permute-done.3 = bf16[286,15,224]{2,0,1:T(8,128)(2,1)} collective-permute-done((bf16[286,15,224]{2,0,1:T(8,128)(2,1)}, bf16[286,15,224]{2,0,1:T(8,128)(2,1)}, u32[]{:S(2)}, u32[]{:S(2)}) %collective-permute-start.3) | collective-permute-done | bytes 1921952 | tf_op jit(solution)/shard_map/ppermute | solution.py:18
  87.1 2.9 copy.12
  89.9 0.0 copy-done.1
  89.9 0.0 copy-start.2
  89.9 15.9 %fusion.14 = f32[286,32,224]{2,1,0:T(8,128)} fusion(bf16[286,15,224]{2,1,0:T(8,128)(2,1)S(1)} %copy.12, bf16[15,32,224]{2,1,0:T(8,128)(2,1)S(1)} %collective-permute-done.1, bf16[256,32,224]{2,1,0:T(8,128)(2,1)S(1)} %copy-done.1, bf16[15,32,224]{2,1,0:T(8,128)(2,1)S(1)} %collective-permute-done, bf16[286,15,224]{2,1,0:T(8,128)(2,1)S(1)} %copy.11, ...), kind=kOutput, calls=%fused_computation.17 | convolution fusion | flops 293931584 | bytes 16144256 | tf_op jit(solution)/shard_map/lqb,qp->lpb/dot_general | solution.py:39
  105.8 0.0 copy-done.2
  105.8 18.1 %divide_subtract_fusion = f32[256,32,224]{0,2,1:T(8,128)S(1)} fusion(bf16[256,32,224]{0,2,1:T(8,128)(2,1)S(1)} %copy-done.2, f32[256,32]{0,1:T(8,128)S(1)} %broadcast_multiply_fusion.1, f32[286,32,224]{2,1,0:T(8,128)} %fusion.14, s32[256]{0:T(256)S(1)} %iota_add_fusion), kind=kOutput, calls=%fused_computation.13 | convolution fusion | flops 6303472128 | bytes 19244032 | tf_op jit(solution)/shard_map/kpb,kl->lpb/dot_general | solution.py:46
  123.9 0.0 copy-start
  123.9 3.0 copy-done
  126.9 1.8 fusion.20
  128.8 0.0 all-reduce.5.cloned.1.call-update
  128.8 9.9 %copy.14 = f32[256,32,224]{2,1,0:T(8,128)} copy(f32[256,32,224]{0,2,1:T(8,128)} %copy-done) | data formatting | bytes 14680064 | tf_op jit(solution)/shard_map/sub | solution.py:64
  138.7 113.2 %all-reduce.5.cloned.1.call-done = f32[224,224]{1,0:T(8,128)} async-done(((f32[224,224]{1,0:T(8,128)}), f32[224,224]{1,0:T(8,128)}) %all-reduce.5.cloned.1.call-update) | async-done | bytes 200720 | tf_op jit(solution)/shard_map/psum | solution.py:68
  251.9 1.6 select_reduce_fusion
  254.1 1.0 select_add_fusion
  255.1 0.1 copy.15
  255.2 1.0 fusion.29
  256.2 11.7 %cholesky.50 = f32[128,128]{1,0:T(8,128)S(1)} custom-call(f32[128,128]{1,0:T(8,128)S(1)} %cholesky.121), custom_call_target="Cholesky" | custom-call | tf_op jit(solution)/shard_map/jit(cholesky)/cholesky | solution.py:71
  268.0 9.8 %custom-call.15 = f32[1,128,128]{1,2,0:T(8,128)S(1)} custom-call(f32[1,128,128]{2,1,0:T(8,128)S(1)} %get-tuple-element.30), custom_call_target="InvertDiagBlocksLowerTriangular" | custom-call | tf_op jit(solution)/shard_map/jit(cholesky)/cholesky | solution.py:71
  277.8 0.2 constant_dynamic-update-slice_fusion.1
  278.0 0.2 convolution_subtract_fusion.1
  278.2 8.8 %cholesky.108 = f32[96,96]{1,0:T(8,128)S(1)} custom-call(f32[96,96]{1,0:T(8,128)S(1)} %convolution_subtract_fusion.1), custom_call_target="Cholesky" | custom-call | tf_op jit(solution)/shard_map/jit(cholesky)/cholesky | solution.py:71
  287.0 0.6 compare_reduce_fusion
  287.6 0.6 compare_reduce_fusion.1
  289.5 0.1 fusion.33
  289.7 19.7 %custom-call.16 = f32[2,128,128]{1,2,0:T(8,128)S(1)} custom-call(f32[2,128,128]{2,1,0:T(8,128)S(1)} %pad_maximum_fusion.1), custom_call_target="InvertDiagBlocksLowerTriangular" | custom-call | tf_op jit(solution)/shard_map/jit(_solve_triangular)/triangular_solve | solution.py:72
  309.3 0.3 fusion.31
  309.6 0.4 convolution_subtract_fusion
  310.0 0.4 fusion.37
  310.4 11.4 %fusion.19 = f32[8192]{0:T(1024)S(1)} fusion(f32[8192,224]{1,0:T(8,128)} %bitcast.37, f32[96,224]{0,1:T(8,128)S(1)} %fusion.37, f32[128,224]{0,1:T(8,128)S(1)} %fusion.31), kind=kOutput, calls=%fused_computation.18 | convolution fusion | flops 4936213504 | bytes 7573504 | tf_op jit(solution)/shard_map/dot_general | solution.py:73
  321.7 0.1 div.39
  321.8 0.7 copy.17
  (15 shorter events, 0.2 us)
Async XLA Ops:
  6.5 245.3 %all-reduce.5.cloned.1.call-start = ((), (), s32[]{:S(2)}) async-start(), calls=%async_computation | async-start | bytes 458752 | tf_op jit(solution)/shard_map/psum | solution.py:68
  15.5 8.6 %collective-permute-start = (bf16[15,32,224]{2,1,0:T(8,128)(2,1)S(1)}, bf16[15,32,224]{2,1,0:T(8,128)(2,1)S(1)}, u32[]{:S(2)}, u32[]{:S(2)}) collective-permute-start(bf16[15,32,224]{2,1,0:T(8,128)(2,1)S(1)} %get-tuple-element.27), channel_id=1, source_target_pairs={{0,8},{8,16},{16,24},{1,9},{9,17},{17,25},{2,10},{10,18},{18,26},{... | collective-permute-start | bytes 645128 | tf_op jit(solution)/shard_map/ppermute | solution.py:15
  19.5 8.4 %collective-permute-start.1 = (bf16[15,32,224]{2,1,0:T(8,128)(2,1)S(1)}, bf16[15,32,224]{2,1,0:T(8,128)(2,1)S(1)}, u32[]{:S(2)}, u32[]{:S(2)}) collective-permute-start(bf16[15,32,224]{2,1,0:T(8,128)(2,1)S(1)} %get-tuple-element.28), channel_id=1, source_target_pairs={{8,0},{16,8},{24,16},{9,1},{17,9},{25,17},{10,2},{18,10},{26,18},{... | collective-permute-start | bytes 645128 | tf_op jit(solution)/shard_map/ppermute | solution.py:18
  32.5 29.1 %collective-permute-start.2 = (bf16[286,15,224]{2,0,1:T(8,128)(2,1)S(1)}, bf16[286,15,224]{2,0,1:T(8,128)(2,1)}, u32[]{:S(2)}, u32[]{:S(2)}) collective-permute-start(bf16[286,15,224]{2,0,1:T(8,128)(2,1)S(1)} %copy.9), channel_id=1, source_target_pairs={{0,1},{1,2},{2,3},{3,4},{4,5},{5,6},{6,7},{8,9},{9,10},{10,11},{11... | collective-permute-start | bytes 5765768 | tf_op jit(solution)/shard_map/ppermute | solution.py:15
  39.6 47.5 %collective-permute-start.3 = (bf16[286,15,224]{2,0,1:T(8,128)(2,1)}, bf16[286,15,224]{2,0,1:T(8,128)(2,1)}, u32[]{:S(2)}, u32[]{:S(2)}) collective-permute-start(bf16[286,15,224]{2,0,1:T(8,128)(2,1)} %copy.10), channel_id=1, source_target_pairs={{1,0},{2,1},{3,2},{4,3},{5,4},{6,5},{7,6},{9,8},{10,9},{11,10},{12... | collective-permute-start | bytes 5765768 | tf_op jit(solution)/shard_map/ppermute | solution.py:18
  41.5 48.4 %copy-start.1 = (bf16[256,32,224]{2,1,0:T(8,128)(2,1)S(1)}, bf16[256,32,224]{2,1,0:T(8,128)(2,1)}, u32[]{:S(2)}) copy-start(bf16[256,32,224]{2,1,0:T(8,128)(2,1)} %copy.6) | copy-start | bytes 11010052
  89.9 15.9 %copy-start.2 = (bf16[256,32,224]{0,2,1:T(8,128)(2,1)S(1)}, bf16[256,32,224]{0,2,1:T(8,128)(2,1)}, u32[]{:S(2)}) copy-start(bf16[256,32,224]{0,2,1:T(8,128)(2,1)} %param.1) | copy-start | bytes 11010052
  123.9 3.0 copy-start
Sparse Core Ops, SparseCore 0:
  128.9 122.8 all-reduce.4
where the time goes:
time: 330 us; the launch traced here: 329 us
  waiting for transfers between devices  163 us (49%)
  other arithmetic  57.8 us (18%)
  matrix products  48.6 us (15%)
  local copies, waits for them, and re-layouts  32.5 us (10%)
  between operations  15.6 us (5%)
  starting transfers between devices  12.1 us (4%)
    psum x1, waiting for transfers between devices, shards(): lax.psum(partial_cov, ('track', 'cross')) / (total_lines * total_pix)  113 us
    another operation x7, other arithmetic, shards(): factor = jnp.linalg.cholesky(loaded)  31.6 us
    ppermute x2, waiting for transfers between devices, with_halo(): lax.ppermute(lax.slice_in_dim(block, 0, width, axis=dim), axis, backward)  26.4 us
    ppermute x2, waiting for transfers between devices, with_halo(): lax.ppermute(lax.slice_in_dim(block, block.shape[dim] - width, None, axis...  23.2 us
    another operation x6, other arithmetic, shards(): inverse = jax.scipy.linalg.solve_triangular(factor, identity, lower=True)  19.8 us
    dot_general x1, matrix products, sum_lines(): jnp.einsum('kpb,kl->lpb', values, weights, precision=precision, preferred...  18.1 us
    dot_general x1, matrix products, sum_pixels(): jnp.einsum('lqb,qp->lpb', values, weights, precision=None, preferred_elem...  15.9 us
    dot_general x1, matrix products, shards(): jnp.dot(flat, inverse.T, precision=highest, preferred_element_type=jnp.fl...  11.4 us
  transfers between devices with their start and end apart: 5, of which 5 were waited for; matrix products, arithmetic and copies ran while one was open for 5% of the time, Pallas kernels for 0%

commit v1 on v0

--- a/solution.py
+++ b/solution.py
@@ -65,7 +65,7 @@
     flat = residual.reshape(lines_dev * pix_dev, bands)
     flat_bf = flat.astype(jnp.bfloat16)
     partial_cov = jnp.dot(flat_bf.T, flat_bf, preferred_element_type=jnp.float32)
-    covariance = lax.psum(partial_cov, ("track", "cross")) / (total_lines * total_pix)
+    covariance = lax.psum(lax.psum(partial_cov, "cross"), "track") / (total_lines * total_pix)
     identity = jnp.eye(bands, dtype=jnp.float32)
     loaded = covariance + LOAD * (jnp.trace(covariance) / bands) * identity
     factor = jnp.linalg.cholesky(loaded)

time: 330 us -> 297 us (0.900)
  waiting for transfers between devices: 163 us -> 127 us
    psum x1 -> x2, waiting for transfers between devices: 113 us -> 77.7 us  [the longest x1 51.5 us: shards(): lax.psum(partial_cov, 'cross')]
  transfers between devices with their start and end apart: 5 -> 6, of which waited for: 5 -> 6; matrix products, arithmetic and copies ran while one was open for 5% -> 5% of each run, Pallas kernels for 0% -> 0%
where the time goes in v1:
time: 297 us; the launch traced here: 294 us
  waiting for transfers between devices  127 us (43%)
  other arithmetic  58.1 us (20%)
  matrix products  48.3 us (16%)
  local copies, waits for them, and re-layouts  32.7 us (11%)
  between operations  15.6 us (5%)
  starting transfers between devices  12.2 us (4%)
    psum x1, waiting for transfers between devices, shards(): lax.psum(partial_cov, 'cross')  51.5 us
    another operation x7, other arithmetic, shards(): factor = jnp.linalg.cholesky(loaded)  31.6 us
    ppermute x2, waiting for transfers between devices, with_halo(): lax.ppermute(lax.slice_in_dim(block, 0, width, axis=dim), axis, backward)  26.4 us
    psum x1, waiting for transfers between devices, shards(): lax.psum(lax.psum(partial_cov, 'cross'), 'track')  26.2 us
    ppermute x2, waiting for transfers between devices, with_halo(): lax.ppermute(lax.slice_in_dim(block, block.shape[dim] - width, None, axis...  23.3 us
    another operation x6, other arithmetic, shards(): inverse = jax.scipy.linalg.solve_triangular(factor, identity, lower=True)  20.1 us
    dot_general x1, matrix products, sum_lines(): jnp.einsum('kpb,kl->lpb', values, weights, precision=precision, preferred...  18.1 us
    dot_general x1, matrix products, sum_pixels(): jnp.einsum('lqb,qp->lpb', values, weights, precision=None, preferred_elem...  15.9 us
  transfers between devices with their start and end apart: 6, of which 6 were waited for; matrix products, arithmetic and copies ran while one was open for 5% of the time, Pallas kernels for 0%

profile of v1, /device:TPU:1, one launch (start us, length us, event | category | flops | bytes accessed | tf_op | source)
XLA Modules:
  0.0 294.2 jit_solution(2207353964549665462)
XLA Ops:
  6.5 0.0 all-reduce.6.cloned.1.call-start
  6.5 7.8 %copy.6 = bf16[256,32,224]{2,1,0:T(8,128)(2,1)} copy(bf16[256,32,224]{0,2,1:T(8,128)(2,1)} %param.1) | data formatting | bytes 7340032 | tf_op args[0]
  14.4 1.1 fusion.46
  15.5 4.0 %collective-permute-start = (bf16[15,32,224]{2,1,0:T(8,128)(2,1)S(1)}, bf16[15,32,224]{2,1,0:T(8,128)(2,1)S(1)}, u32[]{:S(2)}, u32[]{:S(2)}) collective-permute-start(bf16[15,32,224]{2,1,0:T(8,128)(2,1)S(1)} %get-tuple-element.27), channel_id=1, source_target_pairs={{0,8},{8,16},{16,24},{1,9},{9,17},{17,25},{2,10},{10,18},{18,26},{... | collective-permute-start | bytes 645128 | tf_op jit(solution)/shard_map/ppermute | solution.py:15
  19.5 1.3 collective-permute-start.1
  20.8 3.3 %collective-permute-done = bf16[15,32,224]{2,1,0:T(8,128)(2,1)S(1)} collective-permute-done((bf16[15,32,224]{2,1,0:T(8,128)(2,1)S(1)}, bf16[15,32,224]{2,1,0:T(8,128)(2,1)S(1)}, u32[]{:S(2)}, u32[]{:S(2)}) %collective-permute-start) | collective-permute-done | bytes 215072 | tf_op jit(solution)/shard_map/ppermute | solution.py:15
  24.1 3.8 %collective-permute-done.1 = bf16[15,32,224]{2,1,0:T(8,128)(2,1)S(1)} collective-permute-done((bf16[15,32,224]{2,1,0:T(8,128)(2,1)S(1)}, bf16[15,32,224]{2,1,0:T(8,128)(2,1)S(1)}, u32[]{:S(2)}, u32[]{:S(2)}) %collective-permute-start.1) | collective-permute-done | bytes 215072 | tf_op jit(solution)/shard_map/ppermute | solution.py:18
  27.9 2.7 pad_maximum_fusion
  30.7 1.0 fusion.45
  31.7 0.8 copy.9
  32.5 4.9 %collective-permute-start.2 = (bf16[286,15,224]{2,0,1:T(8,128)(2,1)S(1)}, bf16[286,15,224]{2,0,1:T(8,128)(2,1)}, u32[]{:S(2)}, u32[]{:S(2)}) collective-permute-start(bf16[286,15,224]{2,0,1:T(8,128)(2,1)S(1)} %copy.9), channel_id=1, source_target_pairs={{0,1},{1,2},{2,3},{3,4},{4,5},{5,6},{6,7},{8,9},{9,10},{10,11},{11... | collective-permute-start | bytes 5765768 | tf_op jit(solution)/shard_map/ppermute | solution.py:15
  37.4 2.1 copy.10
  39.6 1.9 collective-permute-start.3
  41.5 0.0 copy-start.1
  41.5 0.1 broadcast_multiply_fusion.1
  41.6 20.0 %collective-permute-done.2 = bf16[286,15,224]{2,0,1:T(8,128)(2,1)} collective-permute-done((bf16[286,15,224]{2,0,1:T(8,128)(2,1)S(1)}, bf16[286,15,224]{2,0,1:T(8,128)(2,1)}, u32[]{:S(2)}, u32[]{:S(2)}) %collective-permute-start.2) | collective-permute-done | bytes 1921952 | tf_op jit(solution)/shard_map/ppermute | solution.py:15
  61.6 2.9 copy.11
  64.5 22.6 %collective-permute-done.3 = bf16[286,15,224]{2,0,1:T(8,128)(2,1)} collective-permute-done((bf16[286,15,224]{2,0,1:T(8,128)(2,1)}, bf16[286,15,224]{2,0,1:T(8,128)(2,1)}, u32[]{:S(2)}, u32[]{:S(2)}) %collective-permute-start.3) | collective-permute-done | bytes 1921952 | tf_op jit(solution)/shard_map/ppermute | solution.py:18
  87.1 2.9 copy.12
  89.9 0.0 copy-done.1
  89.9 0.0 copy-start.2
  89.9 15.9 %fusion.14 = f32[286,32,224]{2,1,0:T(8,128)} fusion(bf16[286,15,224]{2,1,0:T(8,128)(2,1)S(1)} %copy.12, bf16[15,32,224]{2,1,0:T(8,128)(2,1)S(1)} %collective-permute-done.1, bf16[256,32,224]{2,1,0:T(8,128)(2,1)S(1)} %copy-done.1, bf16[15,32,224]{2,1,0:T(8,128)(2,1)S(1)} %collective-permute-done, bf16[286,15,224]{2,1,0:T(8,128)(2,1)S(1)} %copy.11, ...), kind=kOutput, calls=%fused_computation.17 | convolution fusion | flops 293931584 | bytes 16144256 | tf_op jit(solution)/shard_map/lqb,qp->lpb/dot_general | solution.py:39
  105.8 0.0 copy-done.2
  105.8 18.1 %divide_subtract_fusion = f32[256,32,224]{0,2,1:T(8,128)S(1)} fusion(bf16[256,32,224]{0,2,1:T(8,128)(2,1)S(1)} %copy-done.2, f32[256,32]{0,1:T(8,128)S(1)} %broadcast_multiply_fusion.1, f32[286,32,224]{2,1,0:T(8,128)} %fusion.14, s32[256]{0:T(256)S(1)} %iota_add_fusion), kind=kOutput, calls=%fused_computation.13 | convolution fusion | flops 6303472128 | bytes 19244032 | tf_op jit(solution)/shard_map/kpb,kl->lpb/dot_general | solution.py:46
  123.9 0.0 copy-start
  123.9 3.0 %copy-done = f32[256,32,224]{0,2,1:T(8,128)} copy-done((f32[256,32,224]{0,2,1:T(8,128)}, f32[256,32,224]{0,2,1:T(8,128)S(1)}, u32[]{:S(2)}) %copy-start) | copy-done | bytes 7340056
  126.9 1.8 fusion.20
  128.8 0.0 all-reduce.6.cloned.1.call-update
  128.8 0.0 all-reduce.8.cloned.1.call-start
  128.9 51.5 %all-reduce.6.cloned.1.call-done = f32[224,224]{1,0:T(8,128)} async-done(((f32[224,224]{1,0:T(8,128)}), f32[224,224]{1,0:T(8,128)}) %all-reduce.6.cloned.1.call-update) | async-done | bytes 200720 | tf_op jit(solution)/shard_map/psum | solution.py:68
  180.4 0.0 all-reduce.8.cloned.1.call-update
  180.4 10.1 %copy.14 = f32[256,32,224]{2,1,0:T(8,128)} copy(f32[256,32,224]{0,2,1:T(8,128)} %copy-done) | data formatting | bytes 14680064 | tf_op jit(solution)/shard_map/sub | solution.py:64
  190.5 26.2 %all-reduce.8.cloned.1.call-done = f32[224,224]{1,0:T(8,128)} async-done(((f32[224,224]{1,0:T(8,128)}), f32[224,224]{1,0:T(8,128)}) %all-reduce.8.cloned.1.call-update) | async-done | bytes 200720 | tf_op jit(solution)/shard_map/psum | solution.py:68
  216.7 1.6 select_reduce_fusion
  219.0 1.0 select_add_fusion
  219.9 0.1 copy.15
  220.1 1.0 fusion.29
  221.1 11.7 %cholesky.50 = f32[128,128]{1,0:T(8,128)S(1)} custom-call(f32[128,128]{1,0:T(8,128)S(1)} %cholesky.121), custom_call_target="Cholesky" | custom-call | tf_op jit(solution)/shard_map/jit(cholesky)/cholesky | solution.py:71
  232.8 9.8 %custom-call.15 = f32[1,128,128]{1,2,0:T(8,128)S(1)} custom-call(f32[1,128,128]{2,1,0:T(8,128)S(1)} %get-tuple-element.30), custom_call_target="InvertDiagBlocksLowerTriangular" | custom-call | tf_op jit(solution)/shard_map/jit(cholesky)/cholesky | solution.py:71
  242.7 0.2 constant_dynamic-update-slice_fusion.1
  242.9 0.2 convolution_subtract_fusion.1
  243.1 8.8 %cholesky.108 = f32[96,96]{1,0:T(8,128)S(1)} custom-call(f32[96,96]{1,0:T(8,128)S(1)} %convolution_subtract_fusion.1), custom_call_target="Cholesky" | custom-call | tf_op jit(solution)/shard_map/jit(cholesky)/cholesky | solution.py:71
  251.9 0.6 compare_reduce_fusion
  252.5 0.6 compare_reduce_fusion.1
  254.4 0.1 fusion.33
  254.5 19.9 %custom-call.16 = f32[2,128,128]{1,2,0:T(8,128)S(1)} custom-call(f32[2,128,128]{2,1,0:T(8,128)S(1)} %pad_maximum_fusion.1), custom_call_target="InvertDiagBlocksLowerTriangular" | custom-call | tf_op jit(solution)/shard_map/jit(_solve_triangular)/triangular_solve | solution.py:72
  274.5 0.3 fusion.31
  274.8 0.4 convolution_subtract_fusion
  275.1 0.4 fusion.37
  275.5 11.1 %fusion.19 = f32[8192]{0:T(1024)S(1)} fusion(f32[8192,224]{1,0:T(8,128)} %bitcast.37, f32[96,224]{0,1:T(8,128)S(1)} %fusion.37, f32[128,224]{0,1:T(8,128)S(1)} %fusion.31), kind=kOutput, calls=%fused_computation.18 | convolution fusion | flops 4936213504 | bytes 7573504 | tf_op jit(solution)/shard_map/dot_general | solution.py:73
  286.6 0.1 div.39
  286.7 0.7 copy.17
  (15 shorter events, 0.2 us)
Async XLA Ops:
  6.5 173.8 %all-reduce.6.cloned.1.call-start = ((), (), s32[]{:S(2)}) async-start(), calls=%async_computation | async-start | bytes 458752 | tf_op jit(solution)/shard_map/psum | solution.py:68
  15.5 8.6 %collective-permute-start = (bf16[15,32,224]{2,1,0:T(8,128)(2,1)S(1)}, bf16[15,32,224]{2,1,0:T(8,128)(2,1)S(1)}, u32[]{:S(2)}, u32[]{:S(2)}) collective-permute-start(bf16[15,32,224]{2,1,0:T(8,128)(2,1)S(1)} %get-tuple-element.27), channel_id=1, source_target_pairs={{0,8},{8,16},{16,24},{1,9},{9,17},{17,25},{2,10},{10,18},{18,26},{... | collective-permute-start | bytes 645128 | tf_op jit(solution)/shard_map/ppermute | solution.py:15
  19.5 8.4 %collective-permute-start.1 = (bf16[15,32,224]{2,1,0:T(8,128)(2,1)S(1)}, bf16[15,32,224]{2,1,0:T(8,128)(2,1)S(1)}, u32[]{:S(2)}, u32[]{:S(2)}) collective-permute-start(bf16[15,32,224]{2,1,0:T(8,128)(2,1)S(1)} %get-tuple-element.28), channel_id=1, source_target_pairs={{8,0},{16,8},{24,16},{9,1},{17,9},{25,17},{10,2},{18,10},{26,18},{... | collective-permute-start | bytes 645128 | tf_op jit(solution)/shard_map/ppermute | solution.py:18
  32.5 29.1 %collective-permute-start.2 = (bf16[286,15,224]{2,0,1:T(8,128)(2,1)S(1)}, bf16[286,15,224]{2,0,1:T(8,128)(2,1)}, u32[]{:S(2)}, u32[]{:S(2)}) collective-permute-start(bf16[286,15,224]{2,0,1:T(8,128)(2,1)S(1)} %copy.9), channel_id=1, source_target_pairs={{0,1},{1,2},{2,3},{3,4},{4,5},{5,6},{6,7},{8,9},{9,10},{10,11},{11... | collective-permute-start | bytes 5765768 | tf_op jit(solution)/shard_map/ppermute | solution.py:15
  39.6 47.5 %collective-permute-start.3 = (bf16[286,15,224]{2,0,1:T(8,128)(2,1)}, bf16[286,15,224]{2,0,1:T(8,128)(2,1)}, u32[]{:S(2)}, u32[]{:S(2)}) collective-permute-start(bf16[286,15,224]{2,0,1:T(8,128)(2,1)} %copy.10), channel_id=1, source_target_pairs={{1,0},{2,1},{3,2},{4,3},{5,4},{6,5},{7,6},{9,8},{10,9},{11,10},{12... | collective-permute-start | bytes 5765768 | tf_op jit(solution)/shard_map/ppermute | solution.py:18
  41.5 48.4 %copy-start.1 = (bf16[256,32,224]{2,1,0:T(8,128)(2,1)S(1)}, bf16[256,32,224]{2,1,0:T(8,128)(2,1)}, u32[]{:S(2)}) copy-start(bf16[256,32,224]{2,1,0:T(8,128)(2,1)} %copy.6) | copy-start | bytes 11010052
  89.9 15.9 %copy-start.2 = (bf16[256,32,224]{0,2,1:T(8,128)(2,1)S(1)}, bf16[256,32,224]{0,2,1:T(8,128)(2,1)}, u32[]{:S(2)}) copy-start(bf16[256,32,224]{0,2,1:T(8,128)(2,1)} %param.1) | copy-start | bytes 11010052
  123.9 3.0 %copy-start = (f32[256,32,224]{0,2,1:T(8,128)}, f32[256,32,224]{0,2,1:T(8,128)S(1)}, u32[]{:S(2)}) copy-start(f32[256,32,224]{0,2,1:T(8,128)S(1)} %divide_subtract_fusion) | copy-start | bytes 22020100
  128.8 88.0 %all-reduce.8.cloned.1.call-start = ((), (), s32[]{:S(2)}) async-start(), calls=%async_computation.1 | async-start | bytes 458752 | tf_op jit(solution)/shard_map/psum | solution.py:68
Sparse Core Ops, SparseCore 0:
  128.9 51.4 all-reduce.5
  182.8 33.8 all-reduce.7
